TPU v7x, 32 devices: a whole 2x2x4 slice. The times are simulated.
32 devices in a mesh: rep: 2 (over x), seq: 4 (over y, core), head: 4 (over z).
Axes of the slice: x: 2, y: 2, z: 4, core: 2. Of those that a mesh axis runs over, the one named last changes fastest.
Arguments:
- query_rows: bfloat16 [2048, 8192], P(('rep', 'seq'), 'head'), parts along dimension 0, may hold values from -128 to 128
- span_kv: bfloat16 [2, 2048, 1024], P(None, ('rep', 'seq'), 'head'), parts along dimension 1, may hold values from -6 to 6
- cache_kv: bfloat16 [2, 4096, 1024], P(None, ('rep', 'seq'), 'head'), parts along dimension 1, may hold values from -6 to 6
- cache_len: int32 [8], P(('rep', 'seq')), parts along dimension 0, may hold values from 1 to 512, 1024 in all
Outputs:
- attended: bfloat16 [2048, 8192], P(('rep', 'seq'), 'head'), parts along dimension 0
There are 2 independent parts, one for each index of `rep`. A program takes and returns all parts, laid end to end along the dimension named above; each array names one. Nothing has to cross between parts.
Inputs may be any that keep to these rules, and one draw needn't show every extreme that they name: `cache_len`: the earlier prompt is the filled slots of the instances in order; every instance has at least one filled slot and some instance is full.
All inputs are finite; a program needn't handle non-finite values. No bound on the sum of `cache_len` on one device may be relied on, other than what follows from the above.
Results may differ from a plain program's by a relative error of at most 0.007.
Values may be sent and summed in bfloat16 or wider, within the bound.
No kernel may reach another device: no remote copies, remote signals or barrier semaphores. Data moves between devices by JAX's collectives and lax.ppermute only.
A program may use at most 64 MiB of HBM per device.

v0:
```python
import jax
import jax.numpy as jnp
from jax import lax
from jax.sharding import PartitionSpec as P

HD = 128


blocked_tag = 1073741824
neg_value = -1e30


def fold_rows(carry_state, queries, positions, block_keys, block_values, block_tags):
    row_count = block_keys.shape[0]
    block_rows = 128
    block_count = row_count // block_rows
    kv_local = block_keys.shape[1] // HD
    key_blocks = block_keys.reshape(block_count, block_rows, kv_local, HD)
    value_blocks = block_values.reshape(block_count, block_rows, kv_local, HD)
    tag_blocks = block_tags.reshape(block_count, block_rows)

    def attend(carry_in, keys_in, values_in, tags_in):
        running_max, running_sum, running_out = carry_in
        scores = jnp.einsum(
            "qkgd,rkd->kgqr", queries, keys_in, preferred_element_type=jnp.float32
        ) * HD ** (-0.5)
        visible = tags_in[None, :] <= positions[:, None]
        scores = jnp.where(visible, scores, jnp.float32(neg_value))
        new_max = jnp.maximum(running_max, jnp.max(scores, axis=-1))
        rescale = jnp.exp(running_max - new_max)
        weights = jnp.where(visible, jnp.exp(scores - new_max[..., None]), jnp.float32(0.0))
        running_sum = running_sum * rescale + jnp.sum(weights, axis=-1)
        running_out = running_out * rescale[..., None] + jnp.einsum(
            "kgqr,rkd->kgqd",
            weights.astype(jnp.bfloat16),
            values_in,
            preferred_element_type=jnp.float32,
        )
        return (new_max, running_sum, running_out)

    def advance(carry_in, block_in):
        keys_in, values_in, tags_in = block_in
        carry_out = attend(carry_in, keys_in, values_in, tags_in)
        return (carry_out, None)

    carry_state, unused = lax.scan(advance, carry_state, (key_blocks, value_blocks, tag_blocks))
    return carry_state


def body(query_rows, span_kv, cache_kv, cache_len):
    tok_rows = query_rows.shape[0]
    kv_width = span_kv.shape[2]
    kv_local = kv_width // HD
    q_group = query_rows.shape[1] // kv_width
    own_index = lax.axis_index("seq")
    positions = own_index * tok_rows + jnp.arange(tok_rows, dtype=jnp.int32)
    queries = query_rows.reshape(tok_rows, kv_local, q_group, HD)
    slot_ids = jnp.arange(cache_kv.shape[1], dtype=jnp.int32)
    cache_tags = jnp.where(slot_ids < cache_len[0], jnp.int32(-1), jnp.int32(blocked_tag))
    carry_state = (
        jnp.full((kv_local, q_group, tok_rows), neg_value, jnp.float32),
        jnp.zeros((kv_local, q_group, tok_rows), jnp.float32),
        jnp.zeros((kv_local, q_group, tok_rows, HD), jnp.float32),
    )
    joined_keys = jnp.concatenate([cache_kv[0], span_kv[0]], axis=0)
    joined_values = jnp.concatenate([cache_kv[1], span_kv[1]], axis=0)
    joined_tags = jnp.concatenate([cache_tags, positions], axis=0)
    carry_state = fold_rows(
        carry_state,
        queries,
        positions,
        lax.all_gather(joined_keys, "seq", axis=0, tiled=True),
        lax.all_gather(joined_values, "seq", axis=0, tiled=True),
        lax.all_gather(joined_tags, "seq", axis=0, tiled=True),
    )
    running_max, running_sum, running_out = carry_state
    result = running_out / running_sum[..., None]
    result = jnp.transpose(result, (2, 0, 1, 3)).reshape(tok_rows, kv_local * q_group * HD)
    return result.astype(jnp.bfloat16)


def solution(mesh):
    in_specs = (
        P(("rep", "seq"), "head"),
        P(None, ("rep", "seq"), "head"),
        P(None, ("rep", "seq"), "head"),
        P(("rep", "seq")),
    )
    out_specs = P(("rep", "seq"), "head")
    return jax.shard_map(body, mesh=mesh, in_specs=in_specs, out_specs=out_specs, check_vma=False)
```

profile of v0, /device:TPU:0, one launch (start us, length us, event | category | flops | bytes accessed | tf_op | source)
XLA Modules:
  0.0 155.0 jit_solution(731224061644751360)
XLA Ops:
  6.5 1.1 slice_bitcast_fusion.2
  7.6 1.1 slice_bitcast_fusion
  8.7 0.8 pad_maximum_fusion.1
  9.5 0.8 pad_maximum_fusion
  11.1 1.3 copy.17
  12.4 1.6 %copy.20 = bf16[256,2,8,128]{3,0,2,1:T(8,128)(2,1)S(1)} copy(bf16[256,2,8,128]{0,3,2,1:T(8,128)(2,1)} %bitcast.62) | data formatting | bytes 2097152
  14.0 6.2 %all-gather = s32[4,1,768]{2,1,0:T(1,128)S(1)} all-gather(s32[1,1,768]{2,1,0:T(1,128)S(1)} %reshape.22), channel_id=1, replica_groups=mesh['rep'=2,'seq'=4,'head'=4] {'seq'}, dimensions={0}, use_global_device_ids=true | all-gather | bytes 15360 | tf_op jit(solution)/shard_map/all_gather | solution.py:74
  20.2 11.8 %all-gather.6.cloned.1.call-done = bf16[3072,256]{1,0:T(8,128)(2,1)} async-done(((bf16[768,256]{1,0:T(8,128)(2,1)}), bf16[3072,256]{1,0:T(8,128)(2,1)}) %all-gather.6.cloned.1.call-update) | async-done | bytes 1572880 | tf_op jit(solution)/shard_map/all_gather | solution.py:73
  32.0 3.5 %reshape.28 = bf16[24,128,2,128]{3,2,1,0:T(2,128)(2,1)} reshape(bf16[3072,256]{1,0:T(8,128)(2,1)} %all-gather.6.cloned.1.call-done) | data formatting | bytes 3145728 | tf_op jit(solution)/shard_map/reshape | solution.py:19
  35.5 17.7 %all-gather.4.cloned.1.call-done = bf16[3072,256]{1,0:T(8,128)(2,1)} async-done(((bf16[768,256]{1,0:T(8,128)(2,1)}), bf16[3072,256]{1,0:T(8,128)(2,1)}) %all-gather.4.cloned.1.call-update) | async-done | bytes 1572880 | tf_op jit(solution)/shard_map/all_gather | solution.py:72
  53.2 3.5 %reshape.27 = bf16[24,128,2,128]{3,2,1,0:T(2,128)(2,1)} reshape(bf16[3072,256]{1,0:T(8,128)(2,1)} %all-gather.4.cloned.1.call-done) | data formatting | bytes 3145728 | tf_op jit(solution)/shard_map/reshape | solution.py:18
  56.8 88.7 %while.15 = (s32[]{:T(128)}, f32[2,8,256]{2,1,0:T(8,128)S(1)}, f32[2,8,256]{2,1,0:T(8,128)S(1)}, f32[2,8,256,128]{3,2,1,0:T(8,128)S(1)}, s32[24,128]{1,0:T(8,128...) while((s32[]{:T(128)}, f32[2,8,256]{2,1,0:T(8,128)S(1)}, ...), condition=%wide.region_3.4_spmd.clone, body=%wide.region_0.3_spmd.clone.sunk | while | flops 276877568 | bytes 12324493 | solution.py:46
  56.9 1.0 constant_dynamic-slice_fusion.4
  58.3 0.5 fusion.32
  58.9 1.5 fusion.34
  60.6 1.0 constant_dynamic-slice_fusion.4
  62.6 1.5 fusion.34
  64.3 1.0 constant_dynamic-slice_fusion.4
  66.3 1.5 fusion.34
  68.0 1.0 constant_dynamic-slice_fusion.4
  70.0 1.5 fusion.34
  71.6 1.0 constant_dynamic-slice_fusion.4
  73.7 1.5 fusion.34
  75.3 1.0 constant_dynamic-slice_fusion.4
  77.4 1.5 fusion.34
  79.0 1.0 constant_dynamic-slice_fusion.4
  81.1 1.5 fusion.34
  82.7 1.0 constant_dynamic-slice_fusion.4
  84.8 1.5 fusion.34
  86.4 1.0 constant_dynamic-slice_fusion.4
  88.5 1.5 fusion.34
  90.1 1.0 constant_dynamic-slice_fusion.4
  92.2 1.5 fusion.34
  93.8 1.0 constant_dynamic-slice_fusion.4
  95.9 1.5 fusion.34
  97.5 1.0 constant_dynamic-slice_fusion.4
  99.5 1.5 fusion.34
  101.2 1.0 constant_dynamic-slice_fusion.4
  103.2 1.5 fusion.34
  104.9 1.0 constant_dynamic-slice_fusion.4
  106.9 1.5 fusion.34
  108.6 1.0 constant_dynamic-slice_fusion.4
  110.6 1.5 fusion.34
  112.3 1.0 constant_dynamic-slice_fusion.4
  114.3 1.5 fusion.34
  116.0 1.0 constant_dynamic-slice_fusion.4
  118.0 1.5 fusion.34
  119.7 1.0 constant_dynamic-slice_fusion.4
  121.7 1.5 fusion.34
  123.4 1.0 constant_dynamic-slice_fusion.4
  125.4 1.5 fusion.34
  127.1 1.0 constant_dynamic-slice_fusion.4
  129.1 1.5 fusion.34
  130.8 1.0 constant_dynamic-slice_fusion.4
  132.8 1.5 fusion.34
  134.5 1.0 constant_dynamic-slice_fusion.4
  136.5 1.5 fusion.34
  138.2 1.0 constant_dynamic-slice_fusion.4
  140.2 1.5 fusion.34
  141.9 1.0 constant_dynamic-slice_fusion.4
  143.9 1.5 fusion.34
  145.5 0.7 fusion.18
  146.2 0.7 copy.22
  146.9 1.2 copy.40
  (204 shorter events, 26.5 us)
Async XLA Ops:
  6.5 4.6 %copy-start = (bf16[256,2048]{1,0:T(8,128)(2,1)S(1)}, bf16[256,2048]{1,0:T(8,128)(2,1)}, u32[]{:S(2)}) copy-start(bf16[256,2048]{1,0:T(8,128)(2,1)} %param.6) | copy-start | bytes 3145732
  6.5 25.5 %all-gather.6.cloned.1.call-start = ((), (), s32[]{:S(2)}) async-start(), calls=%async_computation.1 | async-start | bytes 1966080 | tf_op jit(solution)/shard_map/all_gather | solution.py:73
  9.5 43.8 %all-gather.4.cloned.1.call-start = ((), (), s32[]{:S(2)}) async-start(), calls=%async_computation | async-start | bytes 1966080 | tf_op jit(solution)/shard_map/all_gather | solution.py:72
Sparse Core Ops, SparseCore 0:
  9.6 22.3 all-gather.5
  33.6 19.6 all-gather.3
where the time goes:
time: 156 us; the launch traced here: 155 us
  matrix products  47.6 us (31%)
  local copies, waits for them, and re-layouts  37.6 us (24%)
  waiting for transfers between devices  29.5 us (19%)
  other arithmetic  17.7 us (11%)
  between operations  14.2 us (9%)
  blocking collectives  6.19 us (4%)
  loops' own time  2.08 us (1%)
    dot_general x24, matrix products, attend(): jnp.einsum('kgqr,rkd->kgqd', weights.astype(jnp.bfloat16), values_in, pre...  36.4 us
    dynamic_slice x24, local copies, waits for them, and re-layouts, fold_rows(): lax.scan(advance, carry_state, (key_blocks, value_blocks, tag_blocks))  23.3 us
    all_gather x1, waiting for transfers between devices, body(): lax.all_gather(joined_keys, 'seq', axis=0, tiled=True)  17.7 us
    reduce_sum x24, other arithmetic, attend(): running_sum = running_sum * rescale + jnp.sum(weights, axis=-1)  12.7 us
    all_gather x1, waiting for transfers between devices, body(): lax.all_gather(joined_values, 'seq', axis=0, tiled=True)  11.8 us
    dot_general x24, matrix products, attend(): jnp.einsum('qkgd,rkd->kgqr', queries, keys_in, preferred_element_type=jnp...  11.2 us
    all_gather x1, blocking collectives, body(): lax.all_gather(joined_tags, 'seq', axis=0, tiled=True)  6.19 us
    unnamed x6, local copies, waits for them, and re-layouts  4.17 us
  transfers between devices with their start and end apart: 2, of which 2 were waited for; matrix products, arithmetic and copies ran while one was open for 5% of the time, Pallas kernels for 0%

commit v1 on v0

v1 whole, which is shorter than its diff:
```python
import functools

import jax
import jax.numpy as jnp
from jax import lax
from jax.experimental import pallas as pl
from jax.experimental.pallas import tpu as pltpu
from jax.sharding import PartitionSpec as P

HD = 128
NEG = -1e30
BK_CACHE = 128
BK_SPAN = 128


def attn_kernel(lens_ref, own_ref, q_ref, ck_ref, cv_ref, sk_ref, sv_ref, o_ref, *, n_seq, c_dev, t_rows):
    own = own_ref[0]
    q = q_ref[...]
    scale = HD ** (-0.5)

    def step(start, bk, k_ref, v_ref, carry, limit=None, causal=False):
        m_prev, l_prev, acc_prev = carry
        k = k_ref[pl.ds(start, bk), :]
        v = v_ref[pl.ds(start, bk), :]
        s = lax.dot_general(q, k, (((1,), (1,)), ((), ())), preferred_element_type=jnp.float32) * scale
        if limit is not None:
            cols = lax.broadcasted_iota(jnp.int32, s.shape, 1)
            s = jnp.where(cols < limit, s, NEG)
        if causal:
            cols = lax.broadcasted_iota(jnp.int32, s.shape, 1) + start
            rows = lax.broadcasted_iota(jnp.int32, s.shape, 0) + own * t_rows
            s = jnp.where(cols <= rows, s, NEG)
        m_new = jnp.maximum(m_prev, jnp.max(s, axis=1, keepdims=True))
        alpha = jnp.exp(m_prev - m_new)
        p = jnp.exp(s - m_new)
        l_new = alpha * l_prev + jnp.sum(p, axis=1, keepdims=True)
        acc_new = alpha * acc_prev + jnp.dot(p.astype(v.dtype), v, preferred_element_type=jnp.float32)
        return m_new, l_new, acc_new

    carry = (
        jnp.full((t_rows, 1), NEG, jnp.float32),
        jnp.zeros((t_rows, 1), jnp.float32),
        jnp.zeros((t_rows, HD), jnp.float32),
    )
    for inst in range(n_seq):
        length = lens_ref[inst]
        n_full = length // BK_CACHE
        rem = length - n_full * BK_CACHE
        base = inst * c_dev

        def full_block(b, c, base=base):
            start = pl.multiple_of(base + b * BK_CACHE, BK_CACHE)
            return step(start, BK_CACHE, ck_ref, cv_ref, c)

        carry = lax.fori_loop(0, n_full, full_block, carry)

        def part_block(c, base=base, n_full=n_full, rem=rem):
            start = pl.multiple_of(base + n_full * BK_CACHE, BK_CACHE)
            return step(start, BK_CACHE, ck_ref, cv_ref, c, limit=rem)

        carry = lax.cond(rem > 0, part_block, lambda c: c, carry)

    n_before = own * (t_rows // BK_SPAN)

    def span_block(b, c):
        start = pl.multiple_of(b * BK_SPAN, BK_SPAN)
        return step(start, BK_SPAN, sk_ref, sv_ref, c)

    carry = lax.fori_loop(0, n_before, span_block, carry)
    for d in range(t_rows // BK_SPAN):
        start = pl.multiple_of(own * t_rows + d * BK_SPAN, BK_SPAN)
        carry = step(start, BK_SPAN, sk_ref, sv_ref, carry, causal=True)

    m_fin, l_fin, acc_fin = carry
    o_ref[...] = (acc_fin / l_fin).astype(o_ref.dtype)


def attention(lens, own, q, ck, sk):
    t_rows, q_width = q.shape
    kv_width = ck.shape[2]
    kv_local = kv_width // HD
    group = q_width // kv_width
    n_seq = lens.shape[0]
    c_rows = ck.shape[1]
    s_rows = sk.shape[1]
    c_dev = c_rows // n_seq
    kernel = functools.partial(attn_kernel, n_seq=n_seq, c_dev=c_dev, t_rows=t_rows)
    grid_spec = pltpu.PrefetchScalarGridSpec(
        num_scalar_prefetch=2,
        grid=(kv_local, group),
        in_specs=[
            pl.BlockSpec((t_rows, HD), lambda k, g, *_: (0, k * group + g)),
            pl.BlockSpec((None, c_rows, HD), lambda k, g, *_: (0, 0, k)),
            pl.BlockSpec((None, c_rows, HD), lambda k, g, *_: (1, 0, k)),
            pl.BlockSpec((None, s_rows, HD), lambda k, g, *_: (0, 0, k)),
            pl.BlockSpec((None, s_rows, HD), lambda k, g, *_: (1, 0, k)),
        ],
        out_specs=pl.BlockSpec((t_rows, HD), lambda k, g, *_: (0, k * group + g)),
    )
    return pl.pallas_call(
        kernel,
        out_shape=jax.ShapeDtypeStruct((t_rows, q_width), q.dtype),
        grid_spec=grid_spec,
        compiler_params=pltpu.CompilerParams(dimension_semantics=("arbitrary", "arbitrary")),
    )(lens, own, q, ck, ck, sk, sk)


def body(query_rows, span_kv, cache_kv, cache_len):
    own = lax.axis_index("seq").astype(jnp.int32).reshape(1)
    lens = lax.all_gather(cache_len, "seq", axis=0, tiled=True)
    ck = lax.all_gather(cache_kv, "seq", axis=1, tiled=True)
    sk = lax.all_gather(span_kv, "seq", axis=1, tiled=True)
    return attention(lens, own, query_rows, ck, sk)


def solution(mesh):
    in_specs = (
        P(("rep", "seq"), "head"),
        P(None, ("rep", "seq"), "head"),
        P(None, ("rep", "seq"), "head"),
        P(("rep", "seq")),
    )
    out_specs = P(("rep", "seq"), "head")
    return jax.shard_map(body, mesh=mesh, in_specs=in_specs, out_specs=out_specs, check_vma=False)
```

time: 156 us -> 176 us (1.13)
  the two profiles are of different devices: /device:TPU:0 before, /device:TPU:13 now
where the time goes in v1:
time: 176 us
  Pallas kernels  118 us (67%)
  waiting for transfers between devices  37.5 us (21%)
  between operations  14.1 us (8%)
  blocking collectives  3.71 us (2%)
  local copies, waits for them, and re-layouts  2 us (1%)
    pallas_call x1, Pallas kernels, attention(): pl.pallas_call(kernel, out_shape=jax.ShapeDtypeStruct((t_rows, q_width),...  118 us
    all_gather x1, waiting for transfers between devices, body(): ck = lax.all_gather(cache_kv, 'seq', axis=1, tiled=True)  24.2 us
    all_gather x1, waiting for transfers between devices, body(): sk = lax.all_gather(span_kv, 'seq', axis=1, tiled=True)  11.9 us
    unnamed x1, blocking collectives  3.71 us
  transfers between devices with their start and end apart: 2, of which 2 were waited for; matrix products, arithmetic and copies ran while one was open for 1% of the time, Pallas kernels for 0%

profile of v1, /device:TPU:13, one launch (start us, length us, event | category | flops | bytes accessed | tf_op | source)
XLA Modules:
  0.0 175.7 jit_solution(8260029013385219799)
XLA Ops:
  6.5 0.0 all-gather.5.cloned.1.call-start
  6.5 0.7 all-gather.5.cloned.1.call-update
  7.3 0.0 all-gather.3.cloned.1.call-start
  7.3 0.7 all-gather.3.cloned.1.call-update
  8.7 1.2 dynamic-slice
  9.9 0.8 dynamic-update-slice
  10.7 3.7 %all-reduce.lens_ref = s32[4]{0:T(128)} all-reduce(s32[4]{0:T(128)S(1)} %dynamic-update-slice), channel_id=1, replica_groups=mesh['rep'=2,'seq'=4,'head'=4] {'seq'}, use_global_device_ids=true, to_apply=%add | all-reduce | flops 4 | bytes 32
  14.4 11.9 %all-gather.5.cloned.1.call-done.sk_ref.sv_ref = bf16[2,1024,256]{2,1,0:T(8,128)(2,1)} async-done(((bf16[2,256,256]{2,1,0:T(8,128)(2,1)}), bf16[2,1024,256]{2,1,0:T(8,128)(2,1)}) %all-gather.5.cloned.1.call-update) | async-done | bytes 1048592 | tf_op jit(solution)/shard_map/all_gather | solution.py:112
  26.3 24.2 %all-gather.3.cloned.1.call-done.ck_ref.cv_ref = bf16[2,2048,256]{2,1,0:T(8,128)(2,1)} async-done(((bf16[2,512,256]{2,1,0:T(8,128)(2,1)}), bf16[2,2048,256]{2,1,0:T(8,128)(2,1)}) %all-gather.3.cloned.1.call-update) | async-done | bytes 2097168 | tf_op jit(solution)/shard_map/all_gather | solution.py:111
  50.5 118.4 %shard_map.46 = bf16[256,2048]{1,0:T(8,128)(2,1)} custom-call(s32[4]{0:T(128)} %all-reduce.lens_ref, s32[1]{0:T(128)} %bitcast.1.own_ref, bf16[256,2048]{1,0:T(8,128)(2,1)} %q_ref.1, bf16[2,2048,256]{2,1,0:T(8,128)(2,1)} %all-gather.3.cloned.1.call-done.ck_ref.cv_ref, bf16[2,2048,256]{2,1,0:T(8,128)(2,1)} %all-gather.3.cloned.1.call-done.ck_ref.cv_ref, ...), custom_call_target="tpu_custom_call" | custom-call | tf_op jit(solution)/shard_map/pallas_call | solution.py:100
  (1 shorter events, 0.0 us)
Async XLA Ops:
  6.5 19.7 %all-gather.5.cloned.1.call-start = ((), (), s32[]{:S(2)}) async-start(), calls=%async_computation.1 | async-start | bytes 1310720 | tf_op jit(solution)/shard_map/all_gather | solution.py:112
  7.3 43.2 %all-gather.3.cloned.1.call-start = ((), (), s32[]{:S(2)}) async-start(), calls=%async_computation | async-start | bytes 2621440 | tf_op jit(solution)/shard_map/all_gather | solution.py:111
Sparse Core Ops, SparseCore 0:
  8.9 17.3 all-gather.4
  27.8 22.5 all-gather.2

commit v2 on v1

v2 whole, which is shorter than its diff:
```python
import functools

import jax
import jax.numpy as jnp
from jax import lax
from jax.experimental import pallas as pl
from jax.experimental.pallas import tpu as pltpu
from jax.sharding import PartitionSpec as P

HD = 128
NEG = -1e30
BK = 128


def attn_kernel(lens_ref, own_ref, q_ref, ck_ref, cv_ref, sk_ref, sv_ref, o_ref, m_ref, l_ref, acc_ref, *,
                n_seq, c_dev, t_rows, group):
    own = own_ref[0]
    scale = HD ** (-0.5)
    m_ref[...] = jnp.full(m_ref.shape, NEG, jnp.float32)
    l_ref[...] = jnp.zeros(l_ref.shape, jnp.float32)
    acc_ref[...] = jnp.zeros(acc_ref.shape, jnp.float32)

    def step(start, k_ref, v_ref, limit=None, causal=False):
        k = k_ref[pl.ds(start, BK), :]
        v_t = v_ref[pl.ds(start, BK), :].T
        mask = None
        if limit is not None:
            mask = lax.broadcasted_iota(jnp.int32, (BK, t_rows), 0) < limit
        if causal:
            keys = lax.broadcasted_iota(jnp.int32, (BK, t_rows), 0) + start
            rows = lax.broadcasted_iota(jnp.int32, (BK, t_rows), 1) + own * t_rows
            mask = keys <= rows
        for g in range(group):
            qg = q_ref[:, g * HD:(g + 1) * HD]
            s = lax.dot_general(k, qg, (((1,), (1,)), ((), ())), preferred_element_type=jnp.float32) * scale
            if mask is not None:
                s = jnp.where(mask, s, NEG)
            m_prev = m_ref[g]
            m_new = jnp.maximum(m_prev, jnp.max(s, axis=0, keepdims=True))
            alpha = jnp.exp(m_prev - m_new)
            p = jnp.exp(s - m_new)
            l_ref[g] = alpha * l_ref[g] + jnp.sum(p, axis=0, keepdims=True)
            acc_ref[g] = alpha * acc_ref[g] + jnp.dot(v_t, p.astype(v_t.dtype), preferred_element_type=jnp.float32)
            m_ref[g] = m_new

    def run(n, start_of, k_ref, v_ref):
        def loop_body(b, c):
            step(pl.multiple_of(start_of(b), BK), k_ref, v_ref)
            return c
        lax.fori_loop(0, n, loop_body, 0)

    for inst in range(n_seq):
        length = lens_ref[inst]
        n_full = length // BK
        rem = length - n_full * BK
        base = inst * c_dev
        run(n_full, lambda b, base=base: base + b * BK, ck_ref, cv_ref)

        @pl.when(rem > 0)
        def _(base=base, n_full=n_full, rem=rem):
            step(pl.multiple_of(base + n_full * BK, BK), ck_ref, cv_ref, limit=rem)

    run(own * (t_rows // BK), lambda b: b * BK, sk_ref, sv_ref)
    for d in range(t_rows // BK):
        step(pl.multiple_of(own * t_rows + d * BK, BK), sk_ref, sv_ref, causal=True)

    for g in range(group):
        o_ref[:, g * HD:(g + 1) * HD] = (acc_ref[g] / l_ref[g]).T.astype(o_ref.dtype)


def attention(lens, own, q, ck, sk):
    t_rows, q_width = q.shape
    kv_width = ck.shape[2]
    kv_local = kv_width // HD
    group = q_width // kv_width
    n_seq = lens.shape[0]
    c_rows = ck.shape[1]
    s_rows = sk.shape[1]
    c_dev = c_rows // n_seq
    kernel = functools.partial(attn_kernel, n_seq=n_seq, c_dev=c_dev, t_rows=t_rows, group=group)
    grid_spec = pltpu.PrefetchScalarGridSpec(
        num_scalar_prefetch=2,
        grid=(kv_local,),
        in_specs=[
            pl.BlockSpec((t_rows, group * HD), lambda k, *_: (0, k)),
            pl.BlockSpec((None, c_rows, HD), lambda k, *_: (0, 0, k)),
            pl.BlockSpec((None, c_rows, HD), lambda k, *_: (1, 0, k)),
            pl.BlockSpec((None, s_rows, HD), lambda k, *_: (0, 0, k)),
            pl.BlockSpec((None, s_rows, HD), lambda k, *_: (1, 0, k)),
        ],
        out_specs=pl.BlockSpec((t_rows, group * HD), lambda k, *_: (0, k)),
        scratch_shapes=[
            pltpu.VMEM((group, 1, t_rows), jnp.float32),
            pltpu.VMEM((group, 1, t_rows), jnp.float32),
            pltpu.VMEM((group, HD, t_rows), jnp.float32),
        ],
    )
    return pl.pallas_call(
        kernel,
        out_shape=jax.ShapeDtypeStruct((t_rows, q_width), q.dtype),
        grid_spec=grid_spec,
        compiler_params=pltpu.CompilerParams(dimension_semantics=("arbitrary",)),
    )(lens, own, q, ck, ck, sk, sk)


def body(query_rows, span_kv, cache_kv, cache_len):
    own = lax.axis_index("seq").astype(jnp.int32).reshape(1)
    lens = lax.all_gather(cache_len, "seq", axis=0, tiled=True)
    ck = lax.all_gather(cache_kv, "seq", axis=1, tiled=True)
    sk = lax.all_gather(span_kv, "seq", axis=1, tiled=True)
    return attention(lens, own, query_rows, ck, sk)


def solution(mesh):
    in_specs = (
        P(("rep", "seq"), "head"),
        P(None, ("rep", "seq"), "head"),
        P(None, ("rep", "seq"), "head"),
        P(("rep", "seq")),
    )
    out_specs = P(("rep", "seq"), "head")
    return jax.shard_map(body, mesh=mesh, in_specs=in_specs, out_specs=out_specs, check_vma=False)
```

time: 176 us -> 90.1 us (0.51)
  Pallas kernels: 118 us -> 31.8 us
    pallas_call x1, Pallas kernels: 118 us -> 31.8 us  [attention(): pl.pallas_call(kernel, out_shape=jax.ShapeDtypeStruct((t_rows, q_width),...]
  transfers between devices with their start and end apart: 2 -> 2, of which waited for: 2 -> 2; matrix products, arithmetic and copies ran while one was open for 1% -> 2% of each run, Pallas kernels for 0% -> 0%
where the time goes in v2:
time: 90.1 us; the launch traced here: 89.1 us
  waiting for transfers between devices  37.5 us (42%)
  Pallas kernels  31.8 us (35%)
  between operations  14.1 us (16%)
  blocking collectives  3.71 us (4%)
  local copies, waits for them, and re-layouts  2 us (2%)
    pallas_call x1, Pallas kernels, attention(): pl.pallas_call(kernel, out_shape=jax.ShapeDtypeStruct((t_rows, q_width),...  31.8 us
    all_gather x1, waiting for transfers between devices, body(): ck = lax.all_gather(cache_kv, 'seq', axis=1, tiled=True)  24.2 us
    all_gather x1, waiting for transfers between devices, body(): sk = lax.all_gather(span_kv, 'seq', axis=1, tiled=True)  11.9 us
    unnamed x1, blocking collectives  3.71 us
    unnamed x3, local copies, waits for them, and re-layouts  2 us
  transfers between devices with their start and end apart: 2, of which 2 were waited for; matrix products, arithmetic and copies ran while one was open for 2% of the time, Pallas kernels for 0%

profile of v2, /device:TPU:13, one launch (start us, length us, event | category | flops | bytes accessed | tf_op | source)
XLA Modules:
  0.0 89.1 jit_solution(6976875279057236383)
XLA Ops:
  6.5 0.0 all-gather.5.cloned.1.call-start
  6.5 0.7 all-gather.5.cloned.1.call-update
  7.3 0.0 all-gather.3.cloned.1.call-start
  7.3 0.7 all-gather.3.cloned.1.call-update
  8.7 1.2 %dynamic-slice = u32[1]{0:T(128)} dynamic-slice(u32[32]{0:T(128)} %constant.8, u32[]{:T(128)S(6)} %add), dynamic_slice_sizes={1} | dynamic-slice | bytes 12
  9.9 0.8 dynamic-update-slice
  10.7 3.7 %all-reduce.lens_ref = s32[4]{0:T(128)} all-reduce(s32[4]{0:T(128)S(1)} %dynamic-update-slice), channel_id=1, replica_groups=mesh['rep'=2,'seq'=4,'head'=4] {'seq'}, use_global_device_ids=true, to_apply=%add | all-reduce | flops 4 | bytes 32
  14.4 11.9 %all-gather.5.cloned.1.call-done.sk_ref.sv_ref = bf16[2,1024,256]{2,1,0:T(8,128)(2,1)} async-done(((bf16[2,256,256]{2,1,0:T(8,128)(2,1)}), bf16[2,1024,256]{2,1,0:T(8,128)(2,1)}) %all-gather.5.cloned.1.call-update) | async-done | bytes 1048592 | tf_op jit(solution)/shard_map/all_gather | solution.py:110
  26.3 24.2 %all-gather.3.cloned.1.call-done.ck_ref.cv_ref = bf16[2,2048,256]{2,1,0:T(8,128)(2,1)} async-done(((bf16[2,512,256]{2,1,0:T(8,128)(2,1)}), bf16[2,2048,256]{2,1,0:T(8,128)(2,1)}) %all-gather.3.cloned.1.call-update) | async-done | bytes 2097168 | tf_op jit(solution)/shard_map/all_gather | solution.py:109
  50.5 31.8 %shard_map.46 = bf16[256,2048]{1,0:T(8,128)(2,1)} custom-call(s32[4]{0:T(128)} %all-reduce.lens_ref, s32[1]{0:T(128)} %bitcast.1.own_ref, bf16[256,2048]{1,0:T(8,128)(2,1)} %q_ref.1, bf16[2,2048,256]{2,1,0:T(8,128)(2,1)} %all-gather.3.cloned.1.call-done.ck_ref.cv_ref, bf16[2,2048,256]{2,1,0:T(8,128)(2,1)} %all-gather.3.cloned.1.call-done.ck_ref.cv_ref, ...), custom_call_target="tpu_custom_call" | custom-call | tf_op jit(solution)/shard_map/pallas_call | solution.py:98
  (1 shorter events, 0.0 us)
Async XLA Ops:
  6.5 19.7 %all-gather.5.cloned.1.call-start = ((), (), s32[]{:S(2)}) async-start(), calls=%async_computation.1 | async-start | bytes 1310720 | tf_op jit(solution)/shard_map/all_gather | solution.py:110
  7.3 43.2 %all-gather.3.cloned.1.call-start = ((), (), s32[]{:S(2)}) async-start(), calls=%async_computation | async-start | bytes 2621440 | tf_op jit(solution)/shard_map/all_gather | solution.py:109
Sparse Core Ops, SparseCore 0:
  8.9 17.3 all-gather.4
  27.8 22.5 all-gather.2

commit v3 on v2

v3 whole, which is shorter than its diff:
```python
import functools

import jax
import jax.numpy as jnp
from jax import lax
from jax.experimental import pallas as pl
from jax.experimental.pallas import tpu as pltpu
from jax.sharding import PartitionSpec as P

HD = 128
NEG = -1e30
BK = 256


def step_kernel(sc_ref, q_ref, *refs, ninst, t_rows, group, first, last):
    inst_refs = [refs[4 * i:4 * i + 4] for i in range(ninst)]
    rest = refs[4 * ninst:]
    if first:
        state_in = None
    else:
        state_in, rest = rest[:3], rest[3:]
    qs_ref, m_ref, l_ref, acc_ref = rest[-4:]
    o_refs = rest[:-4]
    own = sc_ref[2 * ninst]
    scale = HD ** (-0.5)
    rows_all = group * t_rows
    reps = BK // 128
    for g in range(group):
        qs_ref[g * t_rows:(g + 1) * t_rows, :] = q_ref[:, g * HD:(g + 1) * HD]
    if first:
        m_ref[...] = jnp.full(m_ref.shape, NEG, jnp.float32)
        l_ref[...] = jnp.zeros(l_ref.shape, jnp.float32)
        acc_ref[...] = jnp.zeros(acc_ref.shape, jnp.float32)
    else:
        m_ref[...] = state_in[0][...]
        l_ref[...] = state_in[1][...]
        acc_ref[...] = state_in[2][...]

    def step(start, k_ref, v_ref, limit=None, causal=False):
        k = k_ref[pl.ds(start, BK), :]
        v = v_ref[pl.ds(start, BK), :]
        s = lax.dot_general(qs_ref[...], k, (((1,), (1,)), ((), ())), preferred_element_type=jnp.float32) * scale
        if limit is not None:
            mask = lax.broadcasted_iota(jnp.int32, (rows_all, BK), 1) < limit
            s = jnp.where(mask, s, NEG)
        if causal:
            cols = lax.broadcasted_iota(jnp.int32, (t_rows, BK), 1) + start
            rows = lax.broadcasted_iota(jnp.int32, (t_rows, BK), 0)
            mask = jnp.concatenate([cols <= rows] * group, axis=0)
            s = jnp.where(mask, s, NEG)
        m_prev = m_ref[...]
        m_new = jnp.maximum(m_prev, jnp.max(s, axis=1, keepdims=True))
        alpha = jnp.exp(m_prev - m_new)
        m_wide = m_new if reps == 1 else jnp.concatenate([m_new] * reps, axis=1)
        p = jnp.exp(s - m_wide)
        p_sum = p[:, :128]
        for r in range(1, reps):
            p_sum = p_sum + p[:, r * 128:(r + 1) * 128]
        l_ref[...] = alpha * l_ref[...] + p_sum
        acc_ref[...] = alpha * acc_ref[...] + jnp.dot(p.astype(v.dtype), v, preferred_element_type=jnp.float32)
        m_ref[...] = m_new

    for i, (ck_ref, cv_ref, sk_ref, sv_ref) in enumerate(inst_refs):
        length = sc_ref[i]
        origin = sc_ref[ninst + i]
        n_full = length // BK
        rem = length - n_full * BK

        def loop_body(b, c, ck_ref=ck_ref, cv_ref=cv_ref):
            step(pl.multiple_of(b * BK, BK), ck_ref, cv_ref)
            return c

        lax.fori_loop(0, n_full, loop_body, 0)

        @pl.when(rem > 0)
        def _(ck_ref=ck_ref, cv_ref=cv_ref, n_full=n_full, rem=rem):
            step(pl.multiple_of(n_full * BK, BK), ck_ref, cv_ref, limit=rem)

        @pl.when(origin < own)
        def _(sk_ref=sk_ref, sv_ref=sv_ref):
            for d in range(t_rows // BK):
                step(d * BK, sk_ref, sv_ref)

        @pl.when(origin == own)
        def _(sk_ref=sk_ref, sv_ref=sv_ref):
            for d in range(t_rows // BK):
                step(d * BK, sk_ref, sv_ref, causal=True)

    if last:
        (o_ref,) = o_refs
        out = acc_ref[...] / jnp.sum(l_ref[...], axis=1, keepdims=True)
        for g in range(group):
            o_ref[:, g * HD:(g + 1) * HD] = out[g * t_rows:(g + 1) * t_rows].astype(o_ref.dtype)
    else:
        o_refs[0][...] = m_ref[...]
        o_refs[1][...] = l_ref[...]
        o_refs[2][...] = acc_ref[...]


def attn_call(sc, q, insts, state, first, last):
    t_rows, q_width = q.shape
    kv_width = insts[0][0].shape[2]
    kv_local = kv_width // HD
    group = q_width // kv_width
    c_rows = insts[0][0].shape[1]
    s_rows = insts[0][1].shape[1]
    rows_all = group * t_rows
    ninst = len(insts)
    kernel = functools.partial(step_kernel, ninst=ninst, t_rows=t_rows, group=group, first=first, last=last)
    st_spec = pl.BlockSpec((rows_all, 128), lambda k, *_: (k, 0))
    st_shape = jax.ShapeDtypeStruct((kv_local * rows_all, 128), jnp.float32)
    in_specs = [pl.BlockSpec((t_rows, group * HD), lambda k, *_: (0, k))]
    args = [sc, q]
    for cache, span in insts:
        in_specs += [
            pl.BlockSpec((None, c_rows, HD), lambda k, *_: (0, 0, k)),
            pl.BlockSpec((None, c_rows, HD), lambda k, *_: (1, 0, k)),
            pl.BlockSpec((None, s_rows, HD), lambda k, *_: (0, 0, k)),
            pl.BlockSpec((None, s_rows, HD), lambda k, *_: (1, 0, k)),
        ]
        args += [cache, cache, span, span]
    if not first:
        in_specs += [st_spec] * 3
        args += list(state)
    if last:
        out_specs = pl.BlockSpec((t_rows, group * HD), lambda k, *_: (0, k))
        out_shape = jax.ShapeDtypeStruct((t_rows, q_width), q.dtype)
    else:
        out_specs = [st_spec] * 3
        out_shape = [st_shape] * 3
    keys = ninst * (c_rows + s_rows)
    heads = kv_local * group
    cost = pl.CostEstimate(
        flops=4 * heads * t_rows * keys * HD,
        transcendentals=heads * t_rows * keys,
        bytes_accessed=2 * t_rows * q_width + 4 * keys * kv_width + 24 * kv_local * rows_all * 128,
    )
    grid_spec = pltpu.PrefetchScalarGridSpec(
        num_scalar_prefetch=1,
        grid=(kv_local,),
        in_specs=in_specs,
        out_specs=out_specs,
        scratch_shapes=[
            pltpu.VMEM((rows_all, HD), q.dtype),
            pltpu.VMEM((rows_all, 128), jnp.float32),
            pltpu.VMEM((rows_all, 128), jnp.float32),
            pltpu.VMEM((rows_all, HD), jnp.float32),
        ],
    )
    return pl.pallas_call(
        kernel,
        out_shape=out_shape,
        grid_spec=grid_spec,
        compiler_params=pltpu.CompilerParams(dimension_semantics=("arbitrary",)),
        cost_estimate=cost,
    )(*args)


def chain_need(n, first_pairs, hops):
    need = []
    for k in range(len(hops)):
        keep = []
        for src in range(n):
            origin = first_pairs[src]
            dst = src
            for j in range(k + 1):
                dst = hops[j](dst)
            later = [dst, dst ^ 1]
            d = dst
            for j in range(k + 1, len(hops)):
                d = hops[j](d)
                later += [d, d ^ 1]
            if any(x > origin for x in later):
                keep.append(src)
        need.append(keep)
    return need


def body(query_rows, span_kv, cache_kv, cache_len):
    n = lax.psum(1, "seq")
    own = lax.axis_index("seq").astype(jnp.int32)
    n_chips = n // 2
    partner = [(i, i ^ 1) for i in range(n)]

    def send(x, fn, keep=None):
        pairs = [(i, fn(i)) for i in range(n) if keep is None or i in keep]
        return lax.ppermute(x, "seq", pairs)

    def to_partner(blk, origin_of, need_span):
        cache, span, length = blk
        keep = [i for i in range(n) if need_span(i)]
        return (send(cache, lambda i: i ^ 1), send(span, lambda i: i ^ 1, keep), send(length, lambda i: i ^ 1))

    local = (cache_kv, span_kv, cache_len)
    part = to_partner(local, None, lambda i: i < (i ^ 1))
    phases = [[(local, own), (part, own ^ 1)]]
    k_right = n_chips // 2
    k_left = n_chips - 1 - k_right
    for sign, count in ((2, k_right), (-2, k_left)):
        blk = local
        for k in range(1, count + 1):
            def hop(i, k=k):
                return (i + sign) % n
            def origin_at(i, k=k):
                return (i - sign * (k - 1)) % n
            keep = []
            for i in range(n):
                o = origin_at(i)
                d = i
                ok = False
                for j in range(k, count + 1):
                    d = (d + sign) % n
                    if d > o or (d ^ 1) > o:
                        ok = True
                if ok:
                    keep.append(i)
            cache, span, length = blk
            blk = (send(cache, hop), send(span, hop, keep), send(length, hop))
            origin = (own - sign * k) % n
            fwd_keep = [i for i in range(n) if (i ^ 1) > (i - sign * k) % n]
            cache, span, length = blk
            fwd = (send(cache, lambda i: i ^ 1), send(span, lambda i: i ^ 1, fwd_keep), send(length, lambda i: i ^ 1))
            phases.append([(blk, origin), (fwd, origin ^ 1)])
    state = None
    for pi, phase in enumerate(phases):
        lens = [b[2].reshape(1) for b, _ in phase]
        origins = [jnp.asarray(o, jnp.int32).reshape(1) for _, o in phase]
        sc = jnp.concatenate(lens + origins + [own.reshape(1)]).astype(jnp.int32)
        insts = [(b[0], b[1]) for b, _ in phase]
        state = attn_call(sc, query_rows, insts, state, first=(pi == 0), last=(pi == len(phases) - 1))
    return state


def solution(mesh):
    in_specs = (
        P(("rep", "seq"), "head"),
        P(None, ("rep", "seq"), "head"),
        P(None, ("rep", "seq"), "head"),
        P(("rep", "seq")),
    )
    out_specs = P(("rep", "seq"), "head")
    return jax.shard_map(body, mesh=mesh, in_specs=in_specs, out_specs=out_specs, check_vma=False)
```

time: 90.1 us -> 60.9 us (0.68)
  waiting for transfers between devices: 37.5 us -> 12.4 us
  between operations: 14.1 us -> 0.8 us
  starting transfers between devices: 0.04 us -> 10.6 us
  blocking collectives: 3.71 us -> 0 us
  local copies, waits for them, and re-layouts: 2 us -> 5.7 us
    all_gather x2 -> x0, waiting for transfers between devices: 36.1 us -> none  [the longest x1 24.2 us: body(): ck = lax.all_gather(cache_kv, 'seq', axis=1, tiled=True)]
    ppermute x0 -> x9, waiting for transfers between devices: none -> 12.4 us  [send(): return lax.ppermute(x, 'seq', pairs)]
    ppermute x0 -> x9, starting transfers between devices: none -> 10.6 us  [send(): return lax.ppermute(x, 'seq', pairs)]
    unnamed x1 -> x0, blocking collectives: 3.71 us -> none
    concatenate x0 -> x2, local copies, waits for them, and re-layouts: none -> 3.35 us  [body(): sc = jnp.concatenate(lens + origins + [own.reshape(1)]).astype(jnp.int32)]
    unnamed x2 -> x0, waiting for transfers between devices: 1.41 us -> none
    pallas_call x1 -> x2, Pallas kernels: 31.8 us -> 31.2 us  [attn_call(): pl.pallas_call(kernel, out_shape=out_shape, grid_spec=grid_spec, compiler...]
    unnamed x3 -> x12, local copies, waits for them, and re-layouts: 2 us -> 2.35 us
  transfers between devices with their start and end apart: 2 -> 9, of which waited for: 2 -> 3; matrix products, arithmetic and copies ran while one was open for 2% -> 6% of each run, Pallas kernels for 0% -> 25%
where the time goes in v3:
time: 60.9 us; the launch traced here: 60.6 us
  Pallas kernels  31.2 us (51%)
  waiting for transfers between devices  12.4 us (20%)
  starting transfers between devices  10.6 us (17%)
  local copies, waits for them, and re-layouts  5.7 us (9%)
  between operations  0.8 us (1%)
    pallas_call x2, Pallas kernels, attn_call(): pl.pallas_call(kernel, out_shape=out_shape, grid_spec=grid_spec, compiler...  31.2 us
    ppermute x9, waiting for transfers between devices, send(): return lax.ppermute(x, 'seq', pairs)  12.4 us
    ppermute x9, starting transfers between devices, send(): return lax.ppermute(x, 'seq', pairs)  10.6 us
    concatenate x2, local copies, waits for them, and re-layouts, body(): sc = jnp.concatenate(lens + origins + [own.reshape(1)]).astype(jnp.int32)  3.35 us
    unnamed x12, local copies, waits for them, and re-layouts  2.35 us
  transfers between devices with their start and end apart: 9, of which 3 were waited for; matrix products, arithmetic and copies ran while one was open for 6% of the time, Pallas kernels for 25%

profile of v3, /device:TPU:13, one launch (start us, length us, event | category | flops | bytes accessed | tf_op | source)
XLA Modules:
  0.0 60.6 jit_solution(4323967887612625829)
XLA Ops:
  0.0 0.2 collective-permute-start.2
  0.2 1.0 %collective-permute-start.7 = (bf16[2,512,256]{2,1,0:T(8,128)(2,1)}, bf16[2,512,256]{2,1,0:T(8,128)(2,1)S(1)}, u32[]{:S(2)}, u32[]{:S(2)}) collective-permute-start(bf16[2,512,256]{2,1,0:T(8,128)(2,1)} %refs_1_.1), channel_id=1, source_target_pairs={{0,4},{4,0},{8,12},{12,8},{1,5},{5,1},{9,13},{13,9},{2,6},{6,2},{1... | collective-permute-start | bytes 1572872 | tf_op jit(solution)/shard_map/ppermute | solution.py:187
  1.2 1.3 %collective-permute-start.3 = (bf16[2,256,256]{2,1,0:T(8,128)(2,1)}, bf16[2,256,256]{2,1,0:T(8,128)(2,1)S(1)}, u32[]{:S(2)}, u32[]{:S(2)}) collective-permute-start(bf16[2,256,256]{2,1,0:T(8,128)(2,1)} %refs_3_.1), channel_id=1, source_target_pairs={{0,8},{4,12},{1,9},{5,13},{2,10},{6,14},{3,11},{7,15},{16,24},{20,... | collective-permute-start | bytes 786440 | tf_op jit(solution)/shard_map/ppermute | solution.py:187
  2.5 1.3 %collective-permute-start.8 = (bf16[2,256,256]{2,1,0:T(8,128)(2,1)}, bf16[2,256,256]{2,1,0:T(8,128)(2,1)S(1)}, u32[]{:S(2)}, u32[]{:S(2)}) collective-permute-start(bf16[2,256,256]{2,1,0:T(8,128)(2,1)} %refs_3_.1), channel_id=1, source_target_pairs={{0,4},{8,12},{1,5},{9,13},{2,6},{10,14},{3,7},{11,15},{16,20},{24,... | collective-permute-start | bytes 786440 | tf_op jit(solution)/shard_map/ppermute | solution.py:187
  3.8 9.2 %collective-permute-done.2.refs_0_.refs_1_ = bf16[2,512,256]{2,1,0:T(8,128)(2,1)S(1)} collective-permute-done((bf16[2,512,256]{2,1,0:T(8,128)(2,1)}, bf16[2,512,256]{2,1,0:T(8,128)(2,1)S(1)}, u32[]{:S(2)}, u32[]{:S(2)}) %collective-permute-start.2) | collective-permute-done | bytes 524320 | tf_op jit(solution)/shard_map/ppermute | solution.py:187
  13.0 0.0 copy-start
  13.0 2.7 %collective-permute-start.4 = (bf16[2,512,256]{2,1,0:T(8,128)(2,1)S(1)}, bf16[2,512,256]{2,1,0:T(8,128)(2,1)S(1)}, u32[]{:S(2)}, u32[]{:S(2)}) collective-permute-start(bf16[2,512,256]{2,1,0:T(8,128)(2,1)S(1)} %collective-permute-done.2.refs_0_.refs_1_), channel_id=1, source_target_pairs={{0,4},{4,0},{8,12},{12,8},{1,5},{5,1},{9,13},{13,9},{2,6},{6,2},{1... | collective-permute-start | bytes 1572872 | tf_op jit(solution)/shard_map/ppermute | solution.py:187
  15.7 0.0 collective-permute-start
  16.4 2.2 %collective-permute-done = s32[1]{0:T(128)} collective-permute-done((s32[1]{0:T(128)}, s32[1]{0:T(128)}, u32[]{:S(2)}, u32[]{:S(2)}) %collective-permute-start) | collective-permute-done | bytes 36 | tf_op jit(solution)/shard_map/ppermute | solution.py:187
  18.6 1.7 %collective-permute-start.6 = (s32[1]{0:T(128)}, s32[1]{0:T(128)}, u32[]{:S(2)}, u32[]{:S(2)}) collective-permute-start(s32[1]{0:T(128)} %param.7), channel_id=1, source_target_pairs={{0,4},{4,0},{8,12},{12,8},{1,5},{5,1},{9,13},{13,9},{2,6},{6,2},{1... | collective-permute-start | bytes 20 | tf_op jit(solution)/shard_map/ppermute | solution.py:187
  20.3 1.0 %collective-permute-done.6 = s32[1]{0:T(128)} collective-permute-done((s32[1]{0:T(128)}, s32[1]{0:T(128)}, u32[]{:S(2)}, u32[]{:S(2)}) %collective-permute-start.6) | collective-permute-done | bytes 36 | tf_op jit(solution)/shard_map/ppermute | solution.py:187
  21.3 0.3 collective-permute-start.1
  21.6 1.4 %concatenate.7.sc_ref = s32[5]{0:T(128)} concatenate(s32[1]{0:T(128)S(6)} %copy.5, s32[1]{0:T(128)} %collective-permute-done.6, s32[1]{0:T(128)} %bitcast.2, s32[1]{0:T(128)} %bitcast.3, s32[1]{0:T(128)} %bitcast.2), dimensions={0} | concatenate | bytes 40 | tf_op jit(solution)/shard_map/concatenate | solution.py:228
  22.9 0.0 collective-permute-done.1
  22.9 2.0 %concatenate.6.sc_ref = s32[5]{0:T(128)} concatenate(s32[1]{0:T(128)} %collective-permute-done, s32[1]{0:T(128)} %collective-permute-done.1, s32[1]{0:T(128)} %bitcast, s32[1]{0:T(128)} %bitcast.1, s32[1]{0:T(128)} %bitcast.2), dimensions={0} | concatenate | bytes 40 | tf_op jit(solution)/shard_map/concatenate | solution.py:228
  24.9 0.0 collective-permute-done.3.refs_2_.refs_3_
  24.9 0.0 copy-start.3
  24.9 2.1 %collective-permute-start.5 = (bf16[2,256,256]{2,1,0:T(8,128)(2,1)S(1)}, bf16[2,256,256]{2,1,0:T(8,128)(2,1)S(1)}, u32[]{:S(2)}, u32[]{:S(2)}) collective-permute-start(bf16[2,256,256]{2,1,0:T(8,128)(2,1)S(1)} %collective-permute-done.3.refs_2_.refs_3_), channel_id=1, source_target_pairs={{8,12},{12,8},{9,13},{13,9},{10,14},{14,10},{11,15},{15,11},{24,28... | collective-permute-start | bytes 786440 | tf_op jit(solution)/shard_map/ppermute | solution.py:187
  27.1 0.0 collective-permute-done.8.refs_6_.refs_7_
  27.1 0.0 copy-start.4
  27.1 0.0 collective-permute-done.7.refs_4_.refs_5_
  27.1 0.7 %copy-done.4 = bf16[2,256,256]{2,1,0:T(8,128)(2,1)} copy-done((bf16[2,256,256]{2,1,0:T(8,128)(2,1)}, bf16[2,256,256]{2,1,0:T(8,128)(2,1)S(1)}, u32[]{:S(2)}) %copy-start.4) | copy-done | bytes 262168
  27.8 0.0 copy-start.1
  27.8 0.8 %copy-done.1 = bf16[2,512,256]{2,1,0:T(8,128)(2,1)} copy-done((bf16[2,512,256]{2,1,0:T(8,128)(2,1)}, bf16[2,512,256]{2,1,0:T(8,128)(2,1)S(1)}, u32[]{:S(2)}) %copy-start.1) | copy-done | bytes 524312
  28.6 15.2 %shard_map.46 = (f32[4096,128]{1,0:T(8,128)}, f32[4096,128]{1,0:T(8,128)}, f32[4096,128]{1,0:T(8,128)}) custom-call(s32[5]{0:T(128)} %concatenate.7.sc_ref, bf16[256,2048]{1,0:T(8,128)(2,1)} %q_ref.3, bf16[2,512,256]{2,1,0:T(8,128)(2,1)} %refs_1_.1, bf16[2,512,256]{2,1,0:T(8,128)(2,1)} %refs_1_.1, bf16[2,256,256]{2,1,0:T(8,128)(2,1)} %refs_3_.1, ...), custom_call_target="tpu_custom_call" | custom-call | flops 3221225472 | bytes 15204352 | tf_op jit(solution)/shard_map/pallas_call | solution.py:150
  43.8 0.0 copy-done
  43.8 0.0 collective-permute-done.5.refs_6_.refs_7_
  43.8 0.0 copy-start.5
  43.8 0.0 collective-permute-done.4.refs_4_.refs_5_
  43.8 0.0 copy-start.2
  43.8 0.0 copy-done.3
  43.8 0.7 %copy-done.5 = bf16[2,256,256]{2,1,0:T(8,128)(2,1)} copy-done((bf16[2,256,256]{2,1,0:T(8,128)(2,1)}, bf16[2,256,256]{2,1,0:T(8,128)(2,1)S(1)}, u32[]{:S(2)}) %copy-start.5) | copy-done | bytes 262168
  44.5 0.2 copy-done.2
  44.7 16.0 %shard_map.47 = bf16[256,2048]{1,0:T(8,128)(2,1)} custom-call(s32[5]{0:T(128)} %concatenate.6.sc_ref, bf16[256,2048]{1,0:T(8,128)(2,1)} %q_ref.3, bf16[2,512,256]{2,1,0:T(8,128)(2,1)} %copy-done, bf16[2,512,256]{2,1,0:T(8,128)(2,1)} %copy-done, bf16[2,256,256]{2,1,0:T(8,128)(2,1)} %copy-done.3, bf16[2,256,256]{2,1,0:T(8,128)(2,1)} %copy-done.3, ...), custom_call_target="tpu_custom_call" | custom-call | flops 3221225472 | bytes 15204352 | tf_op jit(solution)/shard_map/pallas_call | solution.py:150
Async XLA Ops:
  0.0 13.0 %collective-permute-start.2 = (bf16[2,512,256]{2,1,0:T(8,128)(2,1)}, bf16[2,512,256]{2,1,0:T(8,128)(2,1)S(1)}, u32[]{:S(2)}, u32[]{:S(2)}) collective-permute-start(bf16[2,512,256]{2,1,0:T(8,128)(2,1)} %refs_1_.1), channel_id=1, source_target_pairs={{0,8},{4,12},{8,0},{12,4},{1,9},{5,13},{9,1},{13,5},{2,10},{6,14},... | collective-permute-start | bytes 1572872 | tf_op jit(solution)/shard_map/ppermute | solution.py:187
  0.2 26.9 %collective-permute-start.7 = (bf16[2,512,256]{2,1,0:T(8,128)(2,1)}, bf16[2,512,256]{2,1,0:T(8,128)(2,1)S(1)}, u32[]{:S(2)}, u32[]{:S(2)}) collective-permute-start(bf16[2,512,256]{2,1,0:T(8,128)(2,1)} %refs_1_.1), channel_id=1, source_target_pairs={{0,4},{4,0},{8,12},{12,8},{1,5},{5,1},{9,13},{13,9},{2,6},{6,2},{1... | collective-permute-start | bytes 1572872 | tf_op jit(solution)/shard_map/ppermute | solution.py:187
  1.2 23.7 %collective-permute-start.3 = (bf16[2,256,256]{2,1,0:T(8,128)(2,1)}, bf16[2,256,256]{2,1,0:T(8,128)(2,1)S(1)}, u32[]{:S(2)}, u32[]{:S(2)}) collective-permute-start(bf16[2,256,256]{2,1,0:T(8,128)(2,1)} %refs_3_.1), channel_id=1, source_target_pairs={{0,8},{4,12},{1,9},{5,13},{2,10},{6,14},{3,11},{7,15},{16,24},{20,... | collective-permute-start | bytes 786440 | tf_op jit(solution)/shard_map/ppermute | solution.py:187
  2.5 24.6 %collective-permute-start.8 = (bf16[2,256,256]{2,1,0:T(8,128)(2,1)}, bf16[2,256,256]{2,1,0:T(8,128)(2,1)S(1)}, u32[]{:S(2)}, u32[]{:S(2)}) collective-permute-start(bf16[2,256,256]{2,1,0:T(8,128)(2,1)} %refs_3_.1), channel_id=1, source_target_pairs={{0,4},{8,12},{1,5},{9,13},{2,6},{10,14},{3,7},{11,15},{16,20},{24,... | collective-permute-start | bytes 786440 | tf_op jit(solution)/shard_map/ppermute | solution.py:187
  13.0 30.8 %copy-start = (bf16[2,512,256]{2,1,0:T(8,128)(2,1)}, bf16[2,512,256]{2,1,0:T(8,128)(2,1)S(1)}, u32[]{:S(2)}) copy-start(bf16[2,512,256]{2,1,0:T(8,128)(2,1)S(1)} %collective-permute-done.2.refs_0_.refs_1_) | copy-start | bytes 1572868
  13.0 30.8 %collective-permute-start.4 = (bf16[2,512,256]{2,1,0:T(8,128)(2,1)S(1)}, bf16[2,512,256]{2,1,0:T(8,128)(2,1)S(1)}, u32[]{:S(2)}, u32[]{:S(2)}) collective-permute-start(bf16[2,512,256]{2,1,0:T(8,128)(2,1)S(1)} %collective-permute-done.2.refs_0_.refs_1_), channel_id=1, source_target_pairs={{0,4},{4,0},{8,12},{12,8},{1,5},{5,1},{9,13},{13,9},{2,6},{6,2},{1... | collective-permute-start | bytes 1572872 | tf_op jit(solution)/shard_map/ppermute | solution.py:187
  15.7 2.9 %collective-permute-start = (s32[1]{0:T(128)}, s32[1]{0:T(128)}, u32[]{:S(2)}, u32[]{:S(2)}) collective-permute-start(s32[1]{0:T(128)} %param.7), channel_id=1, source_target_pairs={{0,8},{4,12},{8,0},{12,4},{1,9},{5,13},{9,1},{13,5},{2,10},{6,14},... | collective-permute-start | bytes 20 | tf_op jit(solution)/shard_map/ppermute | solution.py:187
  18.6 2.7 %collective-permute-start.6 = (s32[1]{0:T(128)}, s32[1]{0:T(128)}, u32[]{:S(2)}, u32[]{:S(2)}) collective-permute-start(s32[1]{0:T(128)} %param.7), channel_id=1, source_target_pairs={{0,4},{4,0},{8,12},{12,8},{1,5},{5,1},{9,13},{13,9},{2,6},{6,2},{1... | collective-permute-start | bytes 20 | tf_op jit(solution)/shard_map/ppermute | solution.py:187
  21.3 1.7 %collective-permute-start.1 = (s32[1]{0:T(128)}, s32[1]{0:T(128)}, u32[]{:S(2)}, u32[]{:S(2)}) collective-permute-start(s32[1]{0:T(128)} %collective-permute-done), channel_id=1, source_target_pairs={{0,4},{4,0},{8,12},{12,8},{1,5},{5,1},{9,13},{13,9},{2,6},{6,2},{1... | collective-permute-start | bytes 20 | tf_op jit(solution)/shard_map/ppermute | solution.py:187
  24.9 18.9 %copy-start.3 = (bf16[2,256,256]{2,1,0:T(8,128)(2,1)}, bf16[2,256,256]{2,1,0:T(8,128)(2,1)S(1)}, u32[]{:S(2)}) copy-start(bf16[2,256,256]{2,1,0:T(8,128)(2,1)S(1)} %collective-permute-done.3.refs_2_.refs_3_) | copy-start | bytes 786436
  24.9 18.8 %collective-permute-start.5 = (bf16[2,256,256]{2,1,0:T(8,128)(2,1)S(1)}, bf16[2,256,256]{2,1,0:T(8,128)(2,1)S(1)}, u32[]{:S(2)}, u32[]{:S(2)}) collective-permute-start(bf16[2,256,256]{2,1,0:T(8,128)(2,1)S(1)} %collective-permute-done.3.refs_2_.refs_3_), channel_id=1, source_target_pairs={{8,12},{12,8},{9,13},{13,9},{10,14},{14,10},{11,15},{15,11},{24,28... | collective-permute-start | bytes 786440 | tf_op jit(solution)/shard_map/ppermute | solution.py:187
  27.1 0.7 %copy-start.4 = (bf16[2,256,256]{2,1,0:T(8,128)(2,1)}, bf16[2,256,256]{2,1,0:T(8,128)(2,1)S(1)}, u32[]{:S(2)}) copy-start(bf16[2,256,256]{2,1,0:T(8,128)(2,1)S(1)} %collective-permute-done.8.refs_6_.refs_7_) | copy-start | bytes 786436
  27.8 0.8 %copy-start.1 = (bf16[2,512,256]{2,1,0:T(8,128)(2,1)}, bf16[2,512,256]{2,1,0:T(8,128)(2,1)S(1)}, u32[]{:S(2)}) copy-start(bf16[2,512,256]{2,1,0:T(8,128)(2,1)S(1)} %collective-permute-done.7.refs_4_.refs_5_) | copy-start | bytes 1572868
  43.8 0.7 %copy-start.5 = (bf16[2,256,256]{2,1,0:T(8,128)(2,1)}, bf16[2,256,256]{2,1,0:T(8,128)(2,1)S(1)}, u32[]{:S(2)}) copy-start(bf16[2,256,256]{2,1,0:T(8,128)(2,1)S(1)} %collective-permute-done.5.refs_6_.refs_7_) | copy-start | bytes 786436
  43.8 0.9 %copy-start.2 = (bf16[2,512,256]{2,1,0:T(8,128)(2,1)}, bf16[2,512,256]{2,1,0:T(8,128)(2,1)S(1)}, u32[]{:S(2)}) copy-start(bf16[2,512,256]{2,1,0:T(8,128)(2,1)S(1)} %collective-permute-done.4.refs_4_.refs_5_) | copy-start | bytes 1572868
